TPU v7x, 512 devices: a whole 4x8x8 slice. The times are simulated.
512 devices in a mesh: rep: 8 (over y_lo, core), seq: 2 (over y_hi), tp: 32 (over x, z).
Axes of the slice: x: 4, y: 8 (y_hi: 2, y_lo: 4; y = y_hi * 4 + y_lo), z: 8, core: 2. Of those that a mesh axis runs over, the one named last changes fastest.
Arguments:
- hidden: bfloat16 [3072, 8192], P('rep', ('seq', 'tp')), may hold values from -100 to 100
- gain: float32 [8192], replicated, may hold values from 0.1 to 1.9
- w_query: bfloat16 [8192, 8192], P('seq', 'tp'), may hold values from -1 to 1
- w_keyval: bfloat16 [2, 4096, 2048], P(None, 'tp'), may hold values from -1 to 1
- lengths: int32 [8, 2], replicated, may hold values from 128 to 192, as said below
- routes: int32 [8, 2], replicated, may hold values from 0 to 7, as said below
Outputs:
- attended: bfloat16 [3072, 8192], P(('rep', 'seq'), 'tp')
Inputs may be any that keep to these rules, and one draw needn't show every extreme that they name: `routes`: for each j, the responses j of the 8 rollout groups go to 8 different replicas, so each replica receives exactly 2 responses. `lengths`: the responses that one rollout group sends to one replica hold at most 192 tokens together, and in every draw some group sends exactly 192 tokens to one replica.
All inputs are finite; a program needn't handle non-finite values.
Results may differ from a plain program's by a relative error of at most 0.0076.
Values may be sent and summed in bfloat16 or wider, within the bound.
No kernel may reach another device: no remote copies, remote signals or barrier semaphores. Data moves between devices by JAX's collectives and lax.ppermute only.
A program may use at most 64 MiB of HBM per device.

v0:
```python
import math
import jax
import jax.numpy as jnp
from jax import lax
from jax.sharding import PartitionSpec as P

D = 8192
QH = 64
KVH = 8
HD = 128
RESP = 2
LMAX = 192
BUFFER = 384
ROPE_BASE = 500000.0
NORM_EPS = 1e-05
MASK_FILL = -1e30


def response_tables(lengths, routes):
    flat_len = lengths.reshape(-1)
    flat_route = routes.reshape(-1)
    response_ids = jnp.arange(flat_len.shape[0], dtype=jnp.int32)
    group_of = response_ids // RESP
    same_route = flat_route[:, None] == flat_route[None, :]
    same_group = group_of[:, None] == group_of[None, :]
    earlier = response_ids[None, :] < response_ids[:, None]
    dest_off = jnp.sum(jnp.where(same_route & earlier, flat_len[None, :], 0), axis=1)
    pair_off = jnp.sum(jnp.where(same_route & same_group & earlier, flat_len[None, :], 0), axis=1)
    src_start = jnp.sum(jnp.where(same_group & earlier, flat_len[None, :], 0), axis=1)
    return (flat_len, flat_route, group_of, dest_off, pair_off, src_start)


def locate(positions, replica, tables):
    flat_len, flat_route, group_of, dest_off, pair_off, src_start = tables
    response_ids = jnp.arange(flat_len.shape[0], dtype=jnp.int32)
    position_col = positions[:, None]
    inside = (
        (flat_route[None, :] == replica)
        & (dest_off[None, :] <= position_col)
        & (position_col < dest_off[None, :] + flat_len[None, :])
    )
    inside_int = inside.astype(jnp.int32)
    segment = jnp.sum(inside_int * (response_ids[None, :] + 1), axis=1) - 1
    seg_start = jnp.sum(inside_int * dest_off[None, :], axis=1)
    source_group = jnp.sum(inside_int * group_of[None, :], axis=1)
    pair_first = jnp.sum(inside_int * (dest_off - pair_off)[None, :], axis=1)
    source = jnp.sum(inside_int * src_start[None, :], axis=1)
    within = jnp.where(segment >= 0, positions - seg_start, 0)
    return (segment, within, source_group, pair_first, source)


def rotary(values_in, within):
    head_dim = values_in.shape[-1]
    half_dim = head_dim // 2
    freq_index = jnp.arange(half_dim, dtype=jnp.float32)
    inverse = jnp.power(ROPE_BASE, -2.0 * freq_index / head_dim)
    angles = within.astype(jnp.float32)[:, None] * inverse[None, :]
    cosine = jnp.cos(angles)[:, None, :]
    sine_part = jnp.sin(angles)[:, None, :]
    lower_half = values_in[..., :half_dim]
    upper_half = values_in[..., half_dim:]
    return jnp.concatenate(
        [
            lower_half * cosine - upper_half * sine_part,
            upper_half * cosine + lower_half * sine_part,
        ],
        axis=-1,
    )


def fill_rows(table, indices, present):
    taken = jnp.take(table, indices.reshape(-1), axis=0)
    return jnp.where(present.reshape(-1)[:, None], taken, jnp.zeros((), table.dtype))


def local(hidden, gain, w_query, w_keyval, lengths, routes):
    rep_count = lax.axis_size("rep")
    seq_count = lax.axis_size("seq")
    replica = lax.axis_index("rep")
    seq_index = lax.axis_index("seq")
    column = lax.axis_index("tp")
    feature_cols = hidden.shape[1]
    local_rows = BUFFER // seq_count
    capacity = (RESP + rep_count - 1) // rep_count * LMAX
    head_count = w_query.shape[1] // HD
    tables = response_tables(lengths, routes)
    flat_len, flat_route, group_of, dest_off, pair_off, src_start = tables
    my_len = lax.dynamic_slice_in_dim(flat_len, replica * RESP, RESP)
    my_route = lax.dynamic_slice_in_dim(flat_route, replica * RESP, RESP)
    my_pair = lax.dynamic_slice_in_dim(pair_off, replica * RESP, RESP)
    my_start = lax.dynamic_slice_in_dim(src_start, replica * RESP, RESP)
    slot_ids = jnp.arange(capacity, dtype=jnp.int32)
    targets = jnp.arange(rep_count, dtype=jnp.int32)
    block_off = jnp.broadcast_to(slot_ids[None, :], (rep_count, capacity))
    offsets = block_off[:, :, None]
    inside = (
        (my_route[None, None, :] == targets[:, None, None])
        & (my_pair[None, None, :] <= offsets)
        & (offsets < (my_pair + my_len)[None, None, :])
    )
    inside_int = inside.astype(jnp.int32)
    src_rows = jnp.sum(
        inside_int * (my_start[None, None, :] + offsets - my_pair[None, None, :]), axis=2
    )
    src_rows, present = (src_rows, jnp.any(inside, axis=2))
    outgoing = fill_rows(hidden, src_rows, present)
    incoming = lax.all_to_all(outgoing, "rep", split_axis=0, concat_axis=0, tiled=True)
    all_pos = jnp.arange(BUFFER, dtype=jnp.int32)
    segment, within, source_group, pair_first, source = locate(all_pos, replica, tables)
    gathered_idx = jnp.where(segment >= 0, source_group * capacity + all_pos - pair_first, 0)
    assembled = fill_rows(incoming, gathered_idx, segment >= 0)
    local_x = lax.all_to_all(
        assembled.reshape(BUFFER, 1, feature_cols), "seq", split_axis=0, concat_axis=1, tiled=True
    )
    query_pos = seq_index * local_rows + jnp.arange(local_rows, dtype=jnp.int32)
    query_info = locate(query_pos, replica, tables)
    query_seg = query_info[0]
    query_within = query_info[1]
    query_valid = query_seg >= 0
    gain_halves = gain.reshape(seq_count, D // seq_count)
    gain_local = lax.dynamic_slice_in_dim(gain_halves, column * feature_cols, feature_cols, 1)
    kv_head = column * head_count // (QH // KVH)
    query_weights = lax.all_gather(
        w_query.reshape(1, w_query.shape[0], w_query.shape[1]), "seq", axis=0, tiled=True
    )
    feature_piece = lax.all_gather(local_x, "tp", axis=2, tiled=True)
    scaled_piece = (feature_piece.astype(jnp.float32) * gain_halves[None]).astype(jnp.bfloat16)
    query_acc = jnp.einsum(
        "rsn,snf->rf", scaled_piece, query_weights, preferred_element_type=jnp.float32
    )
    squares = jnp.sum(jnp.square(feature_piece.astype(jnp.float32)), axis=(1, 2))
    inverse_rms = lax.rsqrt(squares / D + NORM_EPS)
    queries = rotary(
        inverse_rms[:, None, None] * query_acc.reshape(local_rows, head_count, HD), query_within
    ).astype(jnp.bfloat16)
    scaled_local = (local_x.astype(jnp.float32) * gain_local[None]).astype(jnp.bfloat16)
    kv_partial = jnp.einsum(
        "rsw,swc->rc", scaled_local, w_keyval, preferred_element_type=jnp.float32
    )
    kv_total = lax.psum(kv_partial, "tp")
    head_block = lax.dynamic_slice_in_dim(kv_total, kv_head * 2 * HD, 2 * HD, 1)
    keys = rotary(inverse_rms[:, None, None] * head_block[:, None, :HD], query_within)[:, 0].astype(
        jnp.bfloat16
    )
    values = (inverse_rms[:, None] * head_block[:, HD:]).astype(jnp.bfloat16)
    score_scale = 1.0 / math.sqrt(HD)
    running = jnp.full((local_rows, head_count), MASK_FILL, jnp.float32)
    key_part = lax.all_gather(keys, "seq", axis=0, tiled=True)
    value_part = lax.all_gather(values, "seq", axis=0, tiled=True)
    key_count = key_part.shape[0]
    key_pos = jnp.arange(key_count, dtype=jnp.int32)
    key_seg = locate(key_pos, replica, tables)[0]
    allowed = (key_seg[None, :] == query_seg[:, None]) & query_valid[:, None] & (
        key_pos[None, :] <= query_pos[:, None]
    ) | (key_pos[None, :] == query_pos[:, None])
    scores = (
        jnp.einsum("rhd,kd->rhk", queries, key_part, preferred_element_type=jnp.float32)
        * score_scale
    )
    scores = jnp.where(allowed[:, None, :], scores, MASK_FILL)
    new_max = jnp.maximum(running, jnp.max(scores, axis=2))
    prob_terms = jnp.where(allowed[:, None, :], jnp.exp(scores - new_max[:, :, None]), 0.0)
    totals = jnp.sum(prob_terms, axis=2)
    accum = jnp.einsum(
        "rhk,kd->rhd",
        prob_terms.astype(jnp.bfloat16),
        value_part,
        preferred_element_type=jnp.float32,
    )
    attended = (
        (accum / totals[:, :, None]).reshape(local_rows, head_count * HD).astype(jnp.bfloat16)
    )
    return jnp.where(query_valid[:, None], attended, jnp.zeros((), jnp.bfloat16))


def solution(mesh):
    in_specs = (P("rep", ("seq", "tp")), P(), P("seq", "tp"), P(None, "tp", None), P(), P())
    out_specs = P(("rep", "seq"), "tp")
    return jax.shard_map(local, mesh=mesh, in_specs=in_specs, out_specs=out_specs, check_vma=False)
```

profile of v0, /device:TPU:16, one launch (start us, length us, event | category | flops | bytes accessed | tf_op | source)
XLA Modules:
  0.0 440.9 jit_solution(4229495986316716021)
XLA Ops:
  6.5 0.8 copy.25
  7.5 0.8 copy.24
  8.4 0.2 select_reduce_fusion.7
  9.1 3.5 gather_fusion
  12.7 1.3 select_select_fusion
  14.0 9.1 %all-to-all-start = ((bf16[8,192,128]{2,1,0:T(8,128)(2,1)}), bf16[8,192,128]{2,1,0:T(8,128)(2,1)S(1)}, u32[]{:S(2)}, u32[]{:S(2)}) async-start(bf16[8,192,128]{2,1,0:T(8,128)(2,1)} %select_select_fusion), calls=%async_computation | async-start | bytes 786432 | tf_op jit(solution)/shard_map/all_to_all | solution.py:107
  23.1 0.1 select_reduce_fusion.1
  23.3 9.1 %all-to-all-done = bf16[8,192,128]{2,1,0:T(8,128)(2,1)S(1)} async-done(((bf16[8,192,128]{2,1,0:T(8,128)(2,1)}), bf16[8,192,128]{2,1,0:T(8,128)(2,1)S(1)}, u32[]{:S(2)}, u32[]{:S(2)}) %all-to-all-start) | async-done | bytes 393248 | tf_op jit(solution)/shard_map/all_to_all | solution.py:107
  32.4 1.4 gather_fusion.1
  33.8 0.2 fusion.37
  34.0 0.5 broadcast.494
  34.5 0.7 reduce.4
  35.2 10.6 %all_to_all.27 = bf16[2,2,12288]{2,1,0:T(2,128)(2,1)S(1)} all-to-all(bf16[2,2,12288]{2,1,0:T(2,128)(2,1)S(1)} %reshape.481), channel_id=1, replica_groups=mesh['rep'=8,'seq'=2,'tp'=32] {'seq'}, dimensions={0} | all-to-all | bytes 196608 | tf_op jit(solution)/shard_map/all_to_all | solution.py:112
  45.9 0.7 copy.29
  46.6 0.7 all-gather.8.cloned.1.call-update
  47.6 0.2 fusion.18
  47.8 2.5 convolution_bitcast_fusion
  50.3 0.4 multiply_cosine_fusion.1
  50.7 82.6 %all-gather.6.cloned.1.call-done = bf16[192,2,1,4096]{3,0,1,2:T(8,128)(2,1)} async-done(((bf16[192,2,1,128]{3,0,1,2:T(8,128)(2,1)}), bf16[192,2,1,4096]{3,0,1,2:T(8,128)(2,1)}) %all-gather.6.cloned.1.call-update) | async-done | bytes 3145744 | tf_op jit(solution)/shard_map/all_gather | solution.py:126
  133.3 2.6 fusion
  135.9 111.5 %all-gather.8.cloned.1.call-done = bf16[8192,256]{1,0:T(8,128)(2,1)} async-done(((bf16[4096,256]{1,0:T(8,128)(2,1)}), bf16[8192,256]{1,0:T(8,128)(2,1)}) %all-gather.8.cloned.1.call-update) | async-done | bytes 4194320 | tf_op jit(solution)/shard_map/all_gather | solution.py:123
  247.4 4.1 fusion.7
  251.7 161.3 %all-reduce.2.cloned.1.call-done = f32[192,2048]{1,0:T(8,128)} async-done(((f32[192,2048]{1,0:T(8,128)}), f32[192,2048]{1,0:T(8,128)}) %all-reduce.2.cloned.1.call-update) | async-done | bytes 1572880 | tf_op jit(solution)/shard_map/psum | solution.py:140
  412.9 1.0 fusion.30
  413.9 0.5 fusion.26
  414.5 9.2 %all-gather.2 = bf16[384,1,128]{2,0,1:T(8,128)(2,1)S(1)} all-gather(bf16[192,1,128]{2,0,1:T(8,128)(2,1)S(1)} %pad_maximum_fusion), channel_id=4, replica_groups=mesh['rep'=8,'seq'=2,'tp'=32] {'seq'}, dimensions={0}, use_global_device_ids=true | all-gather | bytes 147456 | tf_op jit(solution)/shard_map/all_gather | solution.py:148
  423.7 0.1 subtract_convert_fusion
  423.9 0.4 fusion.50
  424.3 8.7 %all_gather.15 = bf16[384,128]{1,0:T(8,128)(2,1)S(1)} all-gather(bf16[192,128]{1,0:T(8,128)(2,1)S(1)} %get-tuple-element.19), channel_id=1, replica_groups=mesh['rep'=8,'seq'=2,'tp'=32] {'seq'}, dimensions={0}, use_global_device_ids=true | all-gather | bytes 147456 | tf_op jit(solution)/shard_map/all_gather | solution.py:149
  433.0 0.3 fusion.12
  433.3 0.3 fusion.11
  433.7 0.7 bitcast_select_fusion
  (41 shorter events, 1.4 us)
Async XLA Ops:
  6.5 41.2 %copy-start = (bf16[2,128,2048]{2,1,0:T(8,128)(2,1)S(1)}, bf16[2,128,2048]{2,1,0:T(8,128)(2,1)}, u32[]{:S(2)}) copy-start(bf16[2,128,2048]{2,1,0:T(8,128)(2,1)} %param.9) | copy-start | bytes 3145732
  12.7 34.7 %copy-start.1 = (f32[8192]{0:T(1024)S(1)}, f32[8192]{0:T(1024)}, u32[]{:S(2)}) copy-start(f32[8192]{0:T(1024)} %param.7) | copy-start | bytes 98308
  14.0 18.4 %all-to-all-start = ((bf16[8,192,128]{2,1,0:T(8,128)(2,1)}), bf16[8,192,128]{2,1,0:T(8,128)(2,1)S(1)}, u32[]{:S(2)}, u32[]{:S(2)}) async-start(bf16[8,192,128]{2,1,0:T(8,128)(2,1)} %select_select_fusion), calls=%async_computation | async-start | bytes 786432 | tf_op jit(solution)/shard_map/all_to_all | solution.py:107
  23.1 110.2 %all-gather.6.cloned.1.call-start = ((), (), s32[]{:S(2)}) async-start(), calls=%async_computation.3 | async-start | bytes 3244032 | tf_op jit(solution)/shard_map/all_gather | solution.py:126
  46.6 200.9 %all-gather.8.cloned.1.call-start = ((), (), s32[]{:S(2)}) async-start(), calls=%async_computation.4 | async-start | bytes 6291456 | tf_op jit(solution)/shard_map/all_gather | solution.py:123
  47.3 365.6 %all-reduce.2.cloned.1.call-start = ((), (), s32[]{:S(2)}) async-start(), calls=%async_computation.2 | async-start | bytes 3145728 | tf_op jit(solution)/shard_map/psum | solution.py:140
Sparse Core Ops, SparseCore 0:
  46.7 86.6 all-gather.5
  135.4 111.9 all-gather.7
  250.8 162.0 all-reduce.1
where the time goes:
time: 441 us
  waiting for transfers between devices  365 us (83%)
  blocking collectives  28.5 us (6%)
  between operations  13.4 us (3%)
  starting transfers between devices  9.17 us (2%)
  other arithmetic  9.02 us (2%)
  local copies, waits for them, and re-layouts  8.3 us (2%)
  matrix products  7.34 us (2%)
    psum x1, waiting for transfers between devices, local(): kv_total = lax.psum(kv_partial, 'tp')  161 us
    all_gather x1, waiting for transfers between devices, local(): lax.all_gather(w_query.reshape(1, w_query.shape[0], w_query.shape[1]), 's...  111 us
    all_gather x1, waiting for transfers between devices, local(): feature_piece = lax.all_gather(local_x, 'tp', axis=2, tiled=True)  82.6 us
    all_to_all x1, blocking collectives, local(): lax.all_to_all(assembled.reshape(BUFFER, 1, feature_cols), 'seq', split_a...  10.6 us
    all_gather x1, blocking collectives, local(): key_part = lax.all_gather(keys, 'seq', axis=0, tiled=True)  9.25 us
    all_to_all x1, waiting for transfers between devices, local(): lax.all_to_all(outgoing, 'rep', split_axis=0, concat_axis=0, tiled=True)  9.09 us
    all_to_all x1, starting transfers between devices, local(): lax.all_to_all(outgoing, 'rep', split_axis=0, concat_axis=0, tiled=True)  9.08 us
  transfers between devices with their start and end apart: 4, of which 4 were waited for; matrix products, arithmetic and copies ran while one was open for 2% of the time, Pallas kernels for 0%

commit v1 on v0

--- a/solution.py
+++ b/solution.py
@@ -3,6 +3,7 @@
 import jax.numpy as jnp
 from jax import lax
 from jax.sharding import PartitionSpec as P
+from jax.lax import all_gather
 
 D = 8192
 QH = 64
@@ -145,8 +146,16 @@
     values = (inverse_rms[:, None] * head_block[:, HD:]).astype(jnp.bfloat16)
     score_scale = 1.0 / math.sqrt(HD)
     running = jnp.full((local_rows, head_count), MASK_FILL, jnp.float32)
-    key_part = lax.all_gather(keys, "seq", axis=0, tiled=True)
-    value_part = lax.all_gather(values, "seq", axis=0, tiled=True)
+
+    def follow_series(q_in, z):
+        plain = jnp.split(
+            all_gather(jnp.concatenate([q_in, z], 1), axis_name="seq", axis=0, tiled=True),
+            [q_in.shape[1]],
+            1,
+        )
+        return plain
+
+    key_part, value_part = follow_series(keys, values)
     key_count = key_part.shape[0]
     key_pos = jnp.arange(key_count, dtype=jnp.int32)
     key_seg = locate(key_pos, replica, tables)[0]

time: 441 us -> 434 us (0.984)
  blocking collectives: 28.5 us -> 20.9 us
    all_gather x2 -> x1, blocking collectives: 18 us -> 10.3 us  [follow_series(): all_gather(jnp.concatenate([q_in, z], 1), axis_name='seq', axis=0, tiled=...]
where the time goes in v1:
time: 434 us; the launch traced here: 433 us
  waiting for transfers between devices  365 us (84%)
  blocking collectives  20.9 us (5%)
  between operations  13.4 us (3%)
  starting transfers between devices  9.17 us (2%)
  other arithmetic  9.05 us (2%)
  local copies, waits for them, and re-layouts  8.3 us (2%)
  matrix products  7.34 us (2%)
    psum x1, waiting for transfers between devices, local(): kv_total = lax.psum(kv_partial, 'tp')  161 us
    all_gather x1, waiting for transfers between devices, local(): lax.all_gather(w_query.reshape(1, w_query.shape[0], w_query.shape[1]), 's...  111 us
    all_gather x1, waiting for transfers between devices, local(): feature_piece = lax.all_gather(local_x, 'tp', axis=2, tiled=True)  82.6 us
    all_to_all x1, blocking collectives, local(): lax.all_to_all(assembled.reshape(BUFFER, 1, feature_cols), 'seq', split_a...  10.6 us
    all_gather x1, blocking collectives, follow_series(): all_gather(jnp.concatenate([q_in, z], 1), axis_name='seq', axis=0, tiled=...  10.3 us
    all_to_all x1, waiting for transfers between devices, local(): lax.all_to_all(outgoing, 'rep', split_axis=0, concat_axis=0, tiled=True)  9.09 us
    all_to_all x1, starting transfers between devices, local(): lax.all_to_all(outgoing, 'rep', split_axis=0, concat_axis=0, tiled=True)  9.08 us
  transfers between devices with their start and end apart: 4, of which 4 were waited for; matrix products, arithmetic and copies ran while one was open for 2% of the time, Pallas kernels for 0%

profile of v1, /device:TPU:16, one launch (start us, length us, event | category | flops | bytes accessed | tf_op | source)
XLA Modules:
  0.0 433.3 jit_solution(2389708032764581507)
XLA Ops:
  6.5 0.8 copy.25
  7.5 0.8 copy.24
  8.4 0.2 select_reduce_fusion.7
  9.1 3.5 gather_fusion
  12.7 1.3 select_select_fusion
  14.0 9.1 %all-to-all-start = ((bf16[8,192,128]{2,1,0:T(8,128)(2,1)}), bf16[8,192,128]{2,1,0:T(8,128)(2,1)S(1)}, u32[]{:S(2)}, u32[]{:S(2)}) async-start(bf16[8,192,128]{2,1,0:T(8,128)(2,1)} %select_select_fusion), calls=%async_computation | async-start | bytes 786432 | tf_op jit(solution)/shard_map/all_to_all | solution.py:108
  23.1 0.1 select_reduce_fusion.1
  23.3 9.1 %all-to-all-done = bf16[8,192,128]{2,1,0:T(8,128)(2,1)S(1)} async-done(((bf16[8,192,128]{2,1,0:T(8,128)(2,1)}), bf16[8,192,128]{2,1,0:T(8,128)(2,1)S(1)}, u32[]{:S(2)}, u32[]{:S(2)}) %all-to-all-start) | async-done | bytes 393248 | tf_op jit(solution)/shard_map/all_to_all | solution.py:108
  32.4 1.4 gather_fusion.1
  33.8 0.2 fusion.35
  34.0 0.5 broadcast.494
  34.5 0.7 reduce.4
  35.2 10.6 %all_to_all.27 = bf16[2,2,12288]{2,1,0:T(2,128)(2,1)S(1)} all-to-all(bf16[2,2,12288]{2,1,0:T(2,128)(2,1)S(1)} %reshape.480), channel_id=1, replica_groups=mesh['rep'=8,'seq'=2,'tp'=32] {'seq'}, dimensions={0} | all-to-all | bytes 196608 | tf_op jit(solution)/shard_map/all_to_all | solution.py:113
  45.8 0.1 reshape.481
  45.9 0.7 copy.29
  46.6 0.7 all-gather.7.cloned.1.call-update
  47.6 0.2 fusion.18
  47.8 2.5 convolution_bitcast_fusion
  50.3 0.4 multiply_cosine_fusion.1
  50.7 82.6 %all-gather.5.cloned.1.call-done = bf16[192,2,1,4096]{3,0,1,2:T(8,128)(2,1)} async-done(((bf16[192,2,1,128]{3,0,1,2:T(8,128)(2,1)}), bf16[192,2,1,4096]{3,0,1,2:T(8,128)(2,1)}) %all-gather.5.cloned.1.call-update) | async-done | bytes 3145744 | tf_op jit(solution)/shard_map/all_gather | solution.py:127
  133.3 2.6 fusion
  135.9 111.5 %all-gather.7.cloned.1.call-done = bf16[8192,256]{1,0:T(8,128)(2,1)} async-done(((bf16[4096,256]{1,0:T(8,128)(2,1)}), bf16[8192,256]{1,0:T(8,128)(2,1)}) %all-gather.7.cloned.1.call-update) | async-done | bytes 4194320 | tf_op jit(solution)/shard_map/all_gather | solution.py:124
  247.4 4.1 fusion.7
  251.7 161.3 %all-reduce.2.cloned.1.call-done = f32[192,2048]{1,0:T(8,128)} async-done(((f32[192,2048]{1,0:T(8,128)}), f32[192,2048]{1,0:T(8,128)}) %all-reduce.2.cloned.1.call-update) | async-done | bytes 1572880 | tf_op jit(solution)/shard_map/psum | solution.py:141
  412.9 1.0 fusion.31
  413.9 0.5 fusion.26
  414.5 10.3 %all_gather.11 = bf16[384,256]{1,0:T(8,128)(2,1)S(1)} all-gather(bf16[192,256]{1,0:T(8,128)(2,1)S(1)} %pad_maximum_fusion), channel_id=1, replica_groups=mesh['rep'=8,'seq'=2,'tp'=32] {'seq'}, dimensions={0}, use_global_device_ids=true | all-gather | bytes 294912 | tf_op jit(solution)/shard_map/all_gather | solution.py:152
  424.8 0.1 subtract_convert_fusion
  425.0 0.4 fusion.48
  425.4 0.3 fusion.12
  425.7 0.3 fusion.11
  426.0 0.7 bitcast_select_fusion
  (41 shorter events, 1.3 us)
Async XLA Ops:
  6.5 41.2 %copy-start = (bf16[2,128,2048]{2,1,0:T(8,128)(2,1)S(1)}, bf16[2,128,2048]{2,1,0:T(8,128)(2,1)}, u32[]{:S(2)}) copy-start(bf16[2,128,2048]{2,1,0:T(8,128)(2,1)} %param.9) | copy-start | bytes 3145732
  12.7 34.7 %copy-start.1 = (f32[8192]{0:T(1024)S(1)}, f32[8192]{0:T(1024)}, u32[]{:S(2)}) copy-start(f32[8192]{0:T(1024)} %param.7) | copy-start | bytes 98308
  14.0 18.4 %all-to-all-start = ((bf16[8,192,128]{2,1,0:T(8,128)(2,1)}), bf16[8,192,128]{2,1,0:T(8,128)(2,1)S(1)}, u32[]{:S(2)}, u32[]{:S(2)}) async-start(bf16[8,192,128]{2,1,0:T(8,128)(2,1)} %select_select_fusion), calls=%async_computation | async-start | bytes 786432 | tf_op jit(solution)/shard_map/all_to_all | solution.py:108
  23.1 110.2 %all-gather.5.cloned.1.call-start = ((), (), s32[]{:S(2)}) async-start(), calls=%async_computation.3 | async-start | bytes 3244032 | tf_op jit(solution)/shard_map/all_gather | solution.py:127
  46.6 200.9 %all-gather.7.cloned.1.call-start = ((), (), s32[]{:S(2)}) async-start(), calls=%async_computation.4 | async-start | bytes 6291456 | tf_op jit(solution)/shard_map/all_gather | solution.py:124
  47.3 365.6 %all-reduce.2.cloned.1.call-start = ((), (), s32[]{:S(2)}) async-start(), calls=%async_computation.2 | async-start | bytes 3145728 | tf_op jit(solution)/shard_map/psum | solution.py:141
Sparse Core Ops, SparseCore 0:
  46.7 86.6 all-gather.4
  135.4 111.9 all-gather.6
  250.8 162.0 all-reduce.1
